TPU v7x, 32 devices: a whole 2x2x4 slice. The times are simulated.
32 devices in a mesh: parts: 2 (over y), aux: 4 (over x, core), pair: 4 (over z).
Axes of the slice: x: 2, y: 2, z: 4, core: 2. Of those that a mesh axis runs over, the one named last changes fastest.
Arguments:
- cholesky: bfloat16 [96, 832, 832], P(('parts', 'aux', 'pair')), parts along dimension 0, may hold values from -1.5 to 1.5
- occ_coef: bfloat16 [2, 2, 832, 128], replicated, may hold values from -0.15625 to 0.15625
- vir_coef: bfloat16 [2, 2, 832, 1536], P(None, None, None, 'pair'), may hold values from -0.15625 to 0.15625
- occ_energy: float32 [128], replicated, may hold values from -3 to -0.3
- vir_energy: float32 [1536], replicated, may hold values from 0.2 to 3
- batch_occ: int32 [3], replicated, may hold values from 0 to 127, as said below
Outputs:
- pair_vectors: bfloat16 [96, 128, 2, 1536], P(('parts', 'aux', 'pair')), parts along dimension 0
- amplitudes: float32 [3072, 2, 3, 3, 1536], P(('parts', 'aux'), None, None, None, 'pair'), parts along dimension 0
There are 2 independent parts, one for each index of `parts`. A program takes and returns all parts, laid end to end along the dimension named above; an argument that names none is the same for every part. Nothing has to cross between parts.
Inputs may be any that keep to these rules, and one draw needn't show every extreme that they name: `batch_occ`: 3 distinct occupied indices, the highest occupied spinor 128 - 1 always among them.
All inputs are finite; a program needn't handle non-finite values.
Results may differ from a plain program's by a relative error of at most 0.0064.
Values may be sent and summed in bfloat16 or wider, within the bound.
No kernel may reach another device: no remote copies, remote signals or barrier semaphores. Data moves between devices by JAX's collectives and lax.ppermute only.
A program may use at most 192 MiB of HBM per device.

v0:
```python
import jax
import jax.numpy as jnp
from jax import lax
from jax.sharding import PartitionSpec as P


def complex_rows(half):
    real_part, imag_part = (half[..., :2, :], half[..., 2:, :])
    c0 = jnp.concatenate([real_part, -imag_part], -2)
    c1 = jnp.concatenate([imag_part, real_part], -2)
    return jnp.stack([c0, c1], -3)


def pair_terms(batch_rows, column_rows):
    left = jnp.concatenate([batch_rows[:, :, 0, :], batch_rows[:, :, 1, :]], 0)
    real_right = jnp.concatenate([column_rows[:, :, 0, :], -column_rows[:, :, 1, :]], 0)
    imag_right = jnp.concatenate([column_rows[:, :, 1, :], column_rows[:, :, 0, :]], 0)
    right = jnp.stack([real_right, imag_right], 1)
    return jnp.einsum("pjb,pcia->bcija", left, right, preferred_element_type=jnp.float32)


def on_device(cholesky, occ_coef, vir_coef, occ_energy, vir_energy, batch_occ):
    vectors = cholesky.shape[0]
    orbitals = cholesky.shape[1]
    occupied = occ_coef.shape[3]
    a_width = vir_coef.shape[3]
    n_pair = lax.axis_size("pair")
    n_aux = lax.axis_size("aux")
    n_parts = lax.axis_size("parts")
    rows = 4 * orbitals
    virtuals = n_pair * a_width
    occ_left = jnp.concatenate([occ_coef[0], -occ_coef[1]], 0)
    v_local = vir_coef.reshape(rows, a_width)
    occ_sel = jnp.take(occ_left, batch_occ, axis=2)
    half_sel = jnp.einsum(
        "kmi,pmn->pikn", occ_sel, cholesky, preferred_element_type=jnp.float32
    ).astype(jnp.bfloat16)
    half_sel_all = lax.all_gather(half_sel, ("aux", "pair"), axis=0, tiled=True)
    count = half_sel_all.shape[0]
    batch = half_sel_all.shape[1]
    lhs_sel = complex_rows(half_sel_all).reshape(count * batch * 2, rows)
    sel_own = jnp.dot(lhs_sel, v_local, preferred_element_type=jnp.float32).astype(jnp.bfloat16)
    sel_own = sel_own.reshape(count, batch, 2, a_width)
    n_q = n_parts * n_aux
    rows_q = rows // n_q
    q = lax.axis_index("parts") * n_aux + lax.axis_index("aux")
    piece = lax.dynamic_slice_in_dim(v_local, q * rows_q, rows_q, 0)
    stage1 = lax.all_gather(piece, "pair", axis=0)
    stage2 = lax.all_gather(stage1, ("parts", "aux"), axis=1)
    v_full = stage2.reshape(n_pair, rows, a_width)
    half = jnp.einsum(
        "kmj,pmn->pjkn", occ_left, cholesky, preferred_element_type=jnp.float32
    ).astype(jnp.bfloat16)
    lhs = complex_rows(half).reshape(vectors * occupied * 2, rows)
    full = jnp.einsum("mk,bkn->mbn", lhs, v_full, preferred_element_type=jnp.float32)
    pair_vectors = full.astype(jnp.bfloat16).reshape(vectors, occupied, 2, virtuals)
    a_start = lax.axis_index("pair") * a_width
    b_width = virtuals // n_aux
    b_start = lax.axis_index("aux") * b_width
    sel_full = lax.all_gather(sel_own, "pair", axis=3, tiled=True)
    sel_b = lax.dynamic_slice_in_dim(sel_full, b_start, b_width, 3)
    coulomb = pair_terms(sel_b, sel_own)
    paired = coulomb - jnp.swapaxes(coulomb, 2, 3)
    occ_e = jnp.take(occ_energy, batch_occ)
    vir_first = lax.dynamic_slice_in_dim(vir_energy, a_start, a_width)
    vir_second = lax.dynamic_slice_in_dim(vir_energy, b_start, b_width)
    denominator = (
        (occ_e[:, None] + occ_e[None, :])[None, None, :, :, None]
        - vir_first[None, None, None, None, :]
        - vir_second[:, None, None, None, None]
    )
    return (pair_vectors, paired / denominator)


def solution(mesh):
    return jax.shard_map(
        on_device,
        mesh=mesh,
        in_specs=(
            P(("parts", "aux", "pair"), None, None),
            P(),
            P(None, None, None, "pair"),
            P(),
            P(),
            P(),
        ),
        out_specs=(
            P(("parts", "aux", "pair"), None, None, None),
            P(("parts", "aux"), None, None, None, "pair"),
        ),
        check_vma=False,
    )
```

profile of v0, /device:TPU:0, one launch (start us, length us, event | category | flops | bytes accessed | tf_op | source)
XLA Modules:
  0.0 213.7 jit_solution(11137517444144872280)
XLA Ops:
  7.2 0.0 copy-start
  7.2 0.0 copy-start.7
  7.2 0.0 all-gather.5.cloned.1.call-start
  7.2 1.6 copy-done
  8.9 0.8 constant_dynamic-slice_fusion
  9.6 0.0 all-gather.5.cloned.1.call-update
  9.7 0.0 all-gather.7.cloned.1.call-start
  9.7 35.3 %all-gather.5.cloned.1.call-done = bf16[1664,384]{1,0:T(8,128)(2,1)} async-done(((bf16[416,384]{1,0:T(8,128)(2,1)}), bf16[1664,384]{1,0:T(8,128)(2,1)}) %all-gather.5.cloned.1.call-update) | async-done | bytes 1277968 | tf_op jit(solution)/shard_map/all_gather | solution.py:48
  45.0 0.0 all-gather.7.cloned.1.call-update
  45.1 0.0 copy-done.7
  45.1 0.0 copy-start.9
  45.1 0.1 slice_bitcast_fusion
  45.2 0.0 copy-start.3
  45.2 0.0 copy-start.5
  45.2 0.8 copy-done.3
  46.0 0.1 copy-done.5
  46.1 1.0 pad_maximum_fusion.2
  47.1 2.0 copy.18
  49.1 0.6 gather_fusion
  49.7 0.6 gather_fusion.1
  50.3 3.2 %fusion.10 = bf16[3,3,4,832]{3,2,0,1:T(4,128)(2,1)S(1)} fusion(bf16[3,832,832]{2,1,0:T(8,128)(2,1)} %param.6, bf16[3,4,832]{2,1,0:T(4,128)(2,1)S(1)} %gather_fusion, pred[3]{0:T(512)(128)(4,1)S(1)} %get-tuple-element.7), kind=kOutput, calls=%fused_computation.17 | convolution fusion | flops 49880064 | bytes 4233219 | tf_op jit(solution)/shard_map/kmi,pmn->pikn/dot_general | solution.py:35
  53.5 40.3 %all_gather.22 = bf16[48,3,4,832]{3,2,0,1:T(4,128)(2,1)S(1)} all-gather(bf16[3,3,4,832]{3,2,0,1:T(4,128)(2,1)S(1)} %fusion.10), channel_id=1, replica_groups=mesh['parts'=2,'aux'=4,'pair'=4] {'aux','pair'}, dimensions={0}, use_global_device_ids=true | all-gather | bytes 1018368 | tf_op jit(solution)/shard_map/all_gather | solution.py:38
  93.8 1.3 slice_negate_fusion.1
  95.0 2.2 %maximum_bitcast_fusion.2 = (bf16[48,3,1,4,832]{4,3,0,1,2:T(4,128)(2,1)S(1)}, bf16[48,3,1,4,832]{4,3,0,1,2:T(4,128)(2,1)S(1)}) fusion(bf16[48,3,2,832]{3,2,0,1:T(2,128)(2,1)S(1)} %get-tuple-element.13, bf16[48,3,2,832]{3,2,0,1:T(2,128)(2,1)S(1)} %get-tuple-element.15, bf16[48,3,2,832]{3,2,0,1:T(2,128)(2,1)S(1)} %get-tuple-element.14), kind=kLoop, calls=%fused_computation.18 | loop fusion | flops 3833856 | bytes 3354624 | tf_op jit(solution)/shard_map/stack | solution.py:11
  97.2 1.5 pad_maximum_fusion.1
  98.8 2.0 copy.19
  100.8 4.6 %reshape.87 = bf16[288,3328]{1,0:T(8,128)(2,1)} reshape(bf16[48,3,2,4,832]{4,3,2,1,0:T(4,128)(2,1)} %copy.19) | data formatting | bytes 3833856 | tf_op jit(solution)/shard_map/reshape | solution.py:41
  105.4 2.7 %convolution_convert_fusion.1 = bf16[288,384]{1,0:T(8,128)(2,1)S(1)} fusion(bf16[288,3328]{1,0:T(8,128)(2,1)} %reshape.87, bf16[3328,384]{1,0:T(8,128)(2,1)S(1)} %bitcast.77), kind=kOutput, calls=%fused_computation.15 | convolution fusion | flops 736210944 | bytes 4694016 | tf_op jit(solution)/shard_map/dot_general | solution.py:42
  108.1 0.1 reshape.88
  108.2 0.0 copy-done.8
  108.2 0.1 fusion.26
  108.3 18.8 %all_gather.23 = bf16[48,3,2,1536]{3,0,1,2:T(8,128)(2,1)S(1)} all-gather(bf16[48,3,2,384]{3,0,1,2:T(8,128)(2,1)S(1)} %copy.20), channel_id=1, replica_groups=mesh['parts'=2,'aux'=4,'pair'=4] {'pair'}, dimensions={3}, use_global_device_ids=true | all-gather | bytes 1105920 | tf_op jit(solution)/shard_map/all_gather | solution.py:60
  127.2 0.1 broadcast_add_fusion
  127.3 0.1 broadcast_subtract_fusion.1
  127.4 0.5 broadcast_subtract_fusion
  127.9 1.6 fusion.14
  129.5 4.7 %fusion = f32[384,2,3,3,384]{0,4,2,3,1:T(8,128)} fusion(f32[2,3,384,3,384]{4,2,3,1,0:T(8,128)S(1)} %fusion.14, f32[384,3,3,384]{0,3,1,2:T(8,128)S(1)} %broadcast_subtract_fusion), kind=kLoop, calls=%fused_computation.3 | loop fusion | flops 5308416 | bytes 26542080 | tf_op jit(solution)/shard_map/div | solution.py:72
  134.2 19.8 %copy.24 = f32[384,2,3,3,384]{4,1,3,2,0:T(2,128)} copy(f32[384,2,3,3,384]{0,4,2,3,1:T(8,128)} %fusion) | data formatting | bytes 21233664
  154.0 6.4 %convert_bitcast_fusion = bf16[3,128,4,832]{1,3,0,2:T(8,128)(2,1)S(1)} fusion(bf16[3,832,832]{2,1,0:T(8,128)(2,1)} %param.6, bf16[2,832,128]{2,1,0:T(8,128)(2,1)S(1)} %copy-done.6, bf16[2,832,128]{2,1,0:T(8,128)(2,1)S(1)} %copy-done.4), kind=kOutput, calls=%fused_computation.12 | convolution fusion | flops 2129494016 | bytes 7561216 | tf_op jit(solution)/shard_map/kmj,pmn->pjkn/dot_general | solution.py:51
  160.4 0.3 slice_negate_fusion
  160.7 0.5 maximum_bitcast_fusion
  161.2 2.8 %pad_maximum_fusion = bf16[3,128,2,4,832]{1,4,0,3,2:T(8,128)(2,1)} fusion(bf16[3,128,1,4,832]{1,4,0,3,2:T(8,128)(2,1)S(1)} %get-tuple-element.12, bf16[3,128,1,4,832]{1,4,0,3,2:T(8,128)(2,1)S(1)} %get-tuple-element.11), kind=kLoop, calls=%fused_computation.4 | loop fusion | flops 2555904 | bytes 10223616 | tf_op jit(solution)/shard_map/stack | solution.py:11
  164.0 11.2 %copy.16 = bf16[3,128,2,4,832]{4,3,2,1,0:T(4,128)(2,1)} copy(bf16[3,128,2,4,832]{1,4,0,3,2:T(8,128)(2,1)} %pad_maximum_fusion) | data formatting | bytes 10223616 | tf_op jit(solution)/shard_map/stack | solution.py:11
  175.2 10.2 %reshape.112 = bf16[768,3328,1]{1,0,2:T(8,128)(2,1)} reshape(bf16[3,128,2,4,832]{4,3,2,1,0:T(4,128)(2,1)} %copy.16) | data formatting | bytes 10223616 | tf_op jit(solution)/shard_map/reshape | solution.py:54
  185.4 12.3 %convolution_convert_fusion = bf16[768,4,384]{2,0,1:T(8,128)(2,1)S(1)} fusion(bf16[768,3328,1]{1,0,2:T(8,128)(2,1)} %reshape.112, bf16[4,3328,384]{2,1,0:T(8,128)(2,1)} %all-gather.7.cloned.1.call-done), kind=kOutput, calls=%fused_computation.14 | convolution fusion | flops 7852916736 | bytes 17694720 | tf_op jit(solution)/shard_map/mk,bkn->mbn/dot_general | solution.py:55
  197.7 0.0 copy-start.1
  197.7 3.3 %copy.17 = bf16[768,4,384]{2,1,0:T(4,128)(2,1)} copy(bf16[768,4,384]{2,0,1:T(8,128)(2,1)S(1)} %convolution_convert_fusion) | data formatting | bytes 4718592 | tf_op jit(solution)/shard_map/convert_element_type | solution.py:56
  200.9 5.9 %reshape.86 = bf16[3,128,2,1536]{3,2,1,0:T(2,128)(2,1)} reshape(bf16[768,4,384]{2,1,0:T(4,128)(2,1)} %copy.17) | data formatting | bytes 4718592 | tf_op jit(solution)/shard_map/reshape | solution.py:56
  (18 shorter events, 0.2 us)
Async XLA Ops:
  7.2 1.7 copy-start
  7.2 37.9 %copy-start.7 = (bf16[2,2,832,128]{3,2,1,0:T(8,128)(2,1)S(1)}, bf16[2,2,832,128]{3,2,1,0:T(8,128)(2,1)}, u32[]{:S(2)}) copy-start(bf16[2,2,832,128]{3,2,1,0:T(8,128)(2,1)} %param.7) | copy-start | bytes 2555908
  7.2 37.8 %all-gather.5.cloned.1.call-start = ((), (), s32[]{:S(2)}) async-start(), calls=%async_computation | async-start | bytes 1597440 | tf_op jit(solution)/shard_map/all_gather | solution.py:48
  9.7 175.7 %all-gather.7.cloned.1.call-start = ((), (), s32[]{:S(2)}) async-start(), calls=%async_computation.1 | async-start | bytes 11501568 | tf_op jit(solution)/shard_map/all_gather | solution.py:49
  45.1 4.0 %copy-start.9 = (s32[3]{0:T(128)S(1)}, s32[3]{0:T(128)}, u32[]{:S(2)}) copy-start(s32[3]{0:T(128)} %param.11) | copy-start | bytes 40
  45.2 0.8 copy-start.3
  45.2 0.9 copy-start.5
  46.1 3.6 %copy-start.2 = (f32[128]{0:T(128)S(1)}, f32[128]{0:T(128)}, u32[]{:S(2)}) copy-start(f32[128]{0:T(128)} %param.9) | copy-start | bytes 1540
  105.4 2.8 %copy-start.8 = (f32[1536]{0:T(1024)S(1)}, f32[1536]{0:T(1024)}, u32[]{:S(2)}) copy-start(f32[1536]{0:T(1024)} %param.10) | copy-start | bytes 18436
  134.2 19.8 %copy-start.4 = (bf16[2,832,128]{2,1,0:T(8,128)(2,1)S(1)}, bf16[2,832,128]{2,1,0:T(8,128)(2,1)}, u32[]{:S(2)}) copy-start(bf16[2,832,128]{2,1,0:T(8,128)(2,1)} %copy-done.3) | copy-start | bytes 1277956
  134.2 19.8 %copy-start.6 = (bf16[2,832,128]{2,1,0:T(8,128)(2,1)S(1)}, bf16[2,832,128]{2,1,0:T(8,128)(2,1)}, u32[]{:S(2)}) copy-start(bf16[2,832,128]{2,1,0:T(8,128)(2,1)} %copy-done.5) | copy-start | bytes 1277956
  197.7 9.2 %copy-start.1 = (bf16[2,2,832,384]{3,2,1,0:T(8,128)(2,1)S(1)}, bf16[2,2,832,384]{3,2,1,0:T(8,128)(2,1)}, u32[]{:S(2)}) copy-start(bf16[2,2,832,384]{3,2,1,0:T(8,128)(2,1)} %param.8) | copy-start | bytes 7667716
Sparse Core Ops, SparseCore 0:
  10.2 34.8 all-gather.4
  46.9 64.6 all-gather.6
where the time goes:
time: 215 us; the launch traced here: 214 us
  local copies, waits for them, and re-layouts  63.7 us (30%)
  blocking collectives  59 us (27%)
  waiting for transfers between devices  35.3 us (16%)
  matrix products  26.1 us (12%)
  other arithmetic  15.1 us (7%)
  between operations  14.3 us (7%)
    all_gather x1, blocking collectives, on_device(): half_sel_all = lax.all_gather(half_sel, ('aux', 'pair'), axis=0, tiled=True)  40.3 us
    all_gather x1, waiting for transfers between devices, on_device(): stage1 = lax.all_gather(piece, 'pair', axis=0)  35.3 us
    unnamed x21, local copies, waits for them, and re-layouts  22.4 us
    all_gather x1, blocking collectives, on_device(): sel_full = lax.all_gather(sel_own, 'pair', axis=3, tiled=True)  18.8 us
    another operation x2, local copies, waits for them, and re-layouts, complex_rows(): return jnp.stack([c0, c1], -3)  13.2 us
    dot_general x1, matrix products, on_device(): jnp.einsum('mk,bkn->mbn', lhs, v_full, preferred_element_type=jnp.float32)  12.3 us
    reshape x1, local copies, waits for them, and re-layouts, on_device(): lhs = complex_rows(half).reshape(vectors * occupied * 2, rows)  10.2 us
    another operation x4, other arithmetic, complex_rows(): return jnp.stack([c0, c1], -3)  7.01 us
  transfers between devices with their start and end apart: 2, of which 1 were waited for; matrix products, arithmetic and copies ran while one was open for 38% of the time, Pallas kernels for 0%

commit v1 on v0

--- a/solution.py
+++ b/solution.py
@@ -2,6 +2,7 @@
 import jax.numpy as jnp
 from jax import lax
 from jax.sharding import PartitionSpec as P
+from jax.lax import axis_index, ppermute, psum
 
 
 def complex_rows(half):
@@ -57,7 +58,14 @@
     a_start = lax.axis_index("pair") * a_width
     b_width = virtuals // n_aux
     b_start = lax.axis_index("aux") * b_width
-    sel_full = lax.all_gather(sel_own, "pair", axis=3, tiled=True)
+    buffer = [sel_own]
+    axis_len = psum(1, "pair")
+    for ii in range(1, axis_len):
+        buffer.append(
+            ppermute(buffer[ii - 1], "pair", [(at, (at - 1) % axis_len) for at in range(axis_len)])
+        )
+    b_now = jnp.concatenate(buffer, 3)
+    sel_full = jnp.roll(b_now, axis_index("pair") * sel_own.shape[3], 3)
     sel_b = lax.dynamic_slice_in_dim(sel_full, b_start, b_width, 3)
     coulomb = pair_terms(sel_b, sel_own)
     paired = coulomb - jnp.swapaxes(coulomb, 2, 3)

time: 215 us -> 208 us (0.967)
  blocking collectives: 59 us -> 40.2 us
  starting transfers between devices: 0.08 us -> 4.53 us
  local copies, waits for them, and re-layouts: 63.7 us -> 67.4 us
  waiting for transfers between devices: 35.3 us -> 38.2 us
    all_gather x1 -> x0, blocking collectives: 18.8 us -> none  [on_device(): sel_full = lax.all_gather(sel_own, 'pair', axis=3, tiled=True)]
    ppermute x0 -> x3, starting transfers between devices: none -> 4.45 us  [on_device(): ppermute(buffer[ii - 1], 'pair', [(at, (at - 1) % axis_len) for at in ran...]
    unnamed x21 -> x32, local copies, waits for them, and re-layouts: 22.4 us -> 26 us
    ppermute x0 -> x3, waiting for transfers between devices: none -> 2.87 us  [on_device(): ppermute(buffer[ii - 1], 'pair', [(at, (at - 1) % axis_len) for at in ran...]
    sub x2, other arithmetic: 0.6 us -> 2.93 us  [on_device(): (occ_e[:, None] + occ_e[None, :])[None, None, :, :, None]]
  transfers between devices with their start and end apart: 2 -> 5, of which waited for: 1 -> 2; matrix products, arithmetic and copies ran while one was open for 38% -> 41% of each run, Pallas kernels for 0% -> 0%
where the time goes in v1:
time: 208 us; the launch traced here: 207 us
  local copies, waits for them, and re-layouts  67.4 us (32%)
  blocking collectives  40.2 us (19%)
  waiting for transfers between devices  38.2 us (18%)
  matrix products  25.1 us (12%)
  other arithmetic  17.1 us (8%)
  between operations  14.4 us (7%)
  starting transfers between devices  4.53 us (2%)
    all_gather x1, blocking collectives, on_device(): half_sel_all = lax.all_gather(half_sel, ('aux', 'pair'), axis=0, tiled=True)  40.2 us
    all_gather x1, waiting for transfers between devices, on_device(): stage1 = lax.all_gather(piece, 'pair', axis=0)  35.3 us
    unnamed x32, local copies, waits for them, and re-layouts  26 us
    another operation x2, local copies, waits for them, and re-layouts, complex_rows(): return jnp.stack([c0, c1], -3)  13.1 us
    dot_general x1, matrix products, on_device(): jnp.einsum('mk,bkn->mbn', lhs, v_full, preferred_element_type=jnp.float32)  12.3 us
    reshape x1, local copies, waits for them, and re-layouts, on_device(): lhs = complex_rows(half).reshape(vectors * occupied * 2, rows)  10.3 us
    another operation x4, other arithmetic, complex_rows(): return jnp.stack([c0, c1], -3)  6.91 us
    reshape x1, local copies, waits for them, and re-layouts, on_device(): full.astype(jnp.bfloat16).reshape(vectors, occupied, 2, virtuals)  5.89 us
  transfers between devices with their start and end apart: 5, of which 2 were waited for; matrix products, arithmetic and copies ran while one was open for 41% of the time, Pallas kernels for 0%

profile of v1, /device:TPU:0, one launch (start us, length us, event | category | flops | bytes accessed | tf_op | source)
XLA Modules:
  0.0 207.0 jit_solution(12830497853346937575)
XLA Ops:
  7.2 0.0 all-gather.5.cloned.1.call-start
  7.2 1.6 copy-done
  8.9 0.8 constant_dynamic-slice_fusion
  9.6 0.0 all-gather.5.cloned.1.call-update
  9.7 0.0 all-gather.7.cloned.1.call-start
  9.7 35.3 %all-gather.5.cloned.1.call-done = bf16[1664,384]{1,0:T(8,128)(2,1)} async-done(((bf16[416,384]{1,0:T(8,128)(2,1)}), bf16[1664,384]{1,0:T(8,128)(2,1)}) %all-gather.5.cloned.1.call-update) | async-done | bytes 1277968 | tf_op jit(solution)/shard_map/all_gather | solution.py:49
  45.1 0.1 slice_bitcast_fusion
  45.2 0.8 copy-done.3
  45.9 0.2 copy-done.5
  46.1 1.0 pad_maximum_fusion.2
  47.1 2.0 copy.20
  49.1 0.6 gather_fusion
  49.7 0.6 gather_fusion.1
  50.3 3.2 %fusion.10 = bf16[3,3,4,832]{3,2,0,1:T(4,128)(2,1)S(1)} fusion(bf16[3,832,832]{2,1,0:T(8,128)(2,1)} %param.6, bf16[3,4,832]{2,1,0:T(4,128)(2,1)S(1)} %gather_fusion, pred[3]{0:T(512)(128)(4,1)S(1)} %get-tuple-element.7), kind=kOutput, calls=%fused_computation.17 | convolution fusion | flops 49880064 | bytes 4233219 | tf_op jit(solution)/shard_map/kmi,pmn->pikn/dot_general | solution.py:36
  53.5 40.2 %all_gather.19 = bf16[48,3,4,832]{3,2,0,1:T(4,128)(2,1)S(1)} all-gather(bf16[3,3,4,832]{3,2,0,1:T(4,128)(2,1)S(1)} %fusion.10), channel_id=1, replica_groups=mesh['parts'=2,'aux'=4,'pair'=4] {'aux','pair'}, dimensions={0}, use_global_device_ids=true | all-gather | bytes 1018368 | tf_op jit(solution)/shard_map/all_gather | solution.py:39
  93.8 1.3 slice_negate_fusion.1
  95.0 2.2 %maximum_bitcast_fusion.2 = (bf16[48,3,1,4,832]{4,3,0,1,2:T(4,128)(2,1)S(1)}, bf16[48,3,1,4,832]{4,3,0,1,2:T(4,128)(2,1)S(1)}) fusion(bf16[48,3,2,832]{3,2,0,1:T(2,128)(2,1)S(1)} %get-tuple-element.15, bf16[48,3,2,832]{3,2,0,1:T(2,128)(2,1)S(1)} %get-tuple-element.17, bf16[48,3,2,832]{3,2,0,1:T(2,128)(2,1)S(1)} %get-tuple-element.16), kind=kLoop, calls=%fused_computation.18 | loop fusion | flops 3833856 | bytes 3354624 | tf_op jit(solution)/shard_map/stack | solution.py:12
  97.3 1.5 pad_maximum_fusion.1
  98.8 2.0 copy.21
  100.8 4.6 %reshape.87 = bf16[288,3328]{1,0:T(8,128)(2,1)} reshape(bf16[48,3,2,4,832]{4,3,2,1,0:T(4,128)(2,1)} %copy.21) | data formatting | bytes 3833856 | tf_op jit(solution)/shard_map/reshape | solution.py:42
  105.4 2.7 %convolution_convert_fusion.1 = bf16[288,384]{1,0:T(8,128)(2,1)S(1)} fusion(bf16[288,3328]{1,0:T(8,128)(2,1)} %reshape.87, bf16[3328,384]{1,0:T(8,128)(2,1)S(1)} %bitcast.77), kind=kOutput, calls=%fused_computation.15 | convolution fusion | flops 736210944 | bytes 4694016 | tf_op jit(solution)/shard_map/dot_general | solution.py:43
  108.1 0.1 reshape.88
  108.2 0.7 constant_dynamic-update-slice_fusion.7
  109.0 0.1 fusion.26
  109.0 0.1 broadcast_add_fusion
  109.1 0.1 broadcast_subtract_fusion.1
  109.2 5.3 %convert_bitcast_fusion = bf16[3,128,4,832]{1,3,0,2:T(8,128)(2,1)S(1)} fusion(bf16[3,832,832]{2,1,0:T(8,128)(2,1)} %param.6, bf16[2,832,128]{2,1,0:T(8,128)(2,1)} %copy-done.5, bf16[2,832,128]{2,1,0:T(8,128)(2,1)S(1)} %copy-done.4), kind=kOutput, calls=%fused_computation.12 | convolution fusion | flops 2129494016 | bytes 7561216 | tf_op jit(solution)/shard_map/kmj,pmn->pjkn/dot_general | solution.py:52
  114.5 0.3 slice_negate_fusion
  114.9 0.5 maximum_bitcast_fusion
  115.4 2.7 %pad_maximum_fusion = bf16[3,128,2,4,832]{1,4,0,3,2:T(8,128)(2,1)} fusion(bf16[3,128,1,4,832]{1,4,0,3,2:T(8,128)(2,1)S(1)} %get-tuple-element.14, bf16[3,128,1,4,832]{1,4,0,3,2:T(8,128)(2,1)S(1)} %get-tuple-element.13), kind=kLoop, calls=%fused_computation.4 | loop fusion | flops 2555904 | bytes 10223616 | tf_op jit(solution)/shard_map/stack | solution.py:12
  118.0 2.9 %broadcast_subtract_fusion = f32[384,3,3,384]{0,3,1,2:T(8,128)} fusion(f32[384]{0:T(512)S(1)} %get-tuple-element.29, f32[3,3,384]{2,0,1:T(4,128)S(1)} %broadcast_subtract_fusion.1), kind=kLoop, calls=%fused_computation.9 | loop fusion | flops 1327104 | bytes 5323776 | tf_op jit(solution)/shard_map/sub | solution.py:76
  120.9 0.1 collective-permute-start.1
  121.0 11.0 %copy.18 = bf16[3,128,2,4,832]{4,3,2,1,0:T(4,128)(2,1)} copy(bf16[3,128,2,4,832]{1,4,0,3,2:T(8,128)(2,1)} %pad_maximum_fusion) | data formatting | bytes 10223616 | tf_op jit(solution)/shard_map/stack | solution.py:12
  132.1 10.3 %reshape.112 = bf16[768,3328,1]{1,0,2:T(8,128)(2,1)} reshape(bf16[3,128,2,4,832]{4,3,2,1,0:T(4,128)(2,1)} %copy.18) | data formatting | bytes 10223616 | tf_op jit(solution)/shard_map/reshape | solution.py:55
  142.5 4.4 %collective-permute-start.2 = (bf16[48,3,2,384]{3,0,1,2:T(8,128)(2,1)S(1)}, bf16[48,3,2,384]{3,0,1,2:T(8,128)(2,1)S(1)}, u32[]{:S(2)}, u32[]{:S(2)}) collective-permute-start(bf16[48,3,2,384]{3,0,1,2:T(8,128)(2,1)S(1)} %collective-permute-done.1), channel_id=1, source_target_pairs={{0,3},{1,0},{2,1},{3,2},{4,7},{5,4},{6,5},{7,6},{8,11},{9,8},{10,9... | collective-permute-start | bytes 663560 | tf_op jit(solution)/shard_map/ppermute | solution.py:65
  146.9 1.0 constant_dynamic-update-slice_fusion.6
  147.9 2.9 %collective-permute-done.2 = bf16[48,3,2,384]{3,0,1,2:T(8,128)(2,1)S(1)} collective-permute-done((bf16[48,3,2,384]{3,0,1,2:T(8,128)(2,1)S(1)}, bf16[48,3,2,384]{3,0,1,2:T(8,128)(2,1)S(1)}, u32[]{:S(2)}, u32[]{:S(2)}) %collective-permute-start.2) | collective-permute-done | bytes 221216 | tf_op jit(solution)/shard_map/ppermute | solution.py:65
  150.8 0.1 constant_dynamic-update-slice_fusion.3
  150.9 1.0 constant_dynamic-update-slice_fusion.2
  152.0 0.1 dynamic-slice_bitcast_fusion.1
  152.2 1.6 fusion.14
  153.7 0.4 slice-done
  154.2 0.4 slice-done.1
  154.5 4.5 %fusion = f32[384,2,3,3,384]{0,4,2,3,1:T(8,128)} fusion(f32[2,3,384,3,384]{4,2,3,1,0:T(8,128)S(1)} %fusion.14, f32[384,3,3,384]{0,3,1,2:T(8,128)S(1)} %bitcast.79), kind=kLoop, calls=%fused_computation.3 | loop fusion | flops 5308416 | bytes 26542080 | tf_op jit(solution)/shard_map/div | solution.py:80
  159.0 19.7 %copy.28 = f32[384,2,3,3,384]{4,1,3,2,0:T(2,128)} copy(f32[384,2,3,3,384]{0,4,2,3,1:T(8,128)} %fusion) | data formatting | bytes 21233664
  178.8 12.3 %convolution_convert_fusion = bf16[768,4,384]{2,0,1:T(8,128)(2,1)S(1)} fusion(bf16[768,3328,1]{1,0,2:T(8,128)(2,1)} %reshape.112, bf16[4,3328,384]{2,1,0:T(8,128)(2,1)} %all-gather.7.cloned.1.call-done), kind=kOutput, calls=%fused_computation.14 | convolution fusion | flops 7852916736 | bytes 17694720 | tf_op jit(solution)/shard_map/mk,bkn->mbn/dot_general | solution.py:56
  191.0 3.2 %copy.19 = bf16[768,4,384]{2,1,0:T(4,128)(2,1)} copy(bf16[768,4,384]{2,0,1:T(8,128)(2,1)S(1)} %convolution_convert_fusion) | data formatting | bytes 4718592 | tf_op jit(solution)/shard_map/convert_element_type | solution.py:57
  194.3 5.9 %reshape.86 = bf16[3,128,2,1536]{3,2,1,0:T(2,128)(2,1)} reshape(bf16[768,4,384]{2,1,0:T(4,128)(2,1)} %copy.19) | data formatting | bytes 4718592 | tf_op jit(solution)/shard_map/reshape | solution.py:57
  (35 shorter events, 0.4 us)
Async XLA Ops:
  7.2 1.7 copy-start
  7.2 37.9 %copy-start.6 = (bf16[2,2,832,128]{3,2,1,0:T(8,128)(2,1)S(1)}, bf16[2,2,832,128]{3,2,1,0:T(8,128)(2,1)}, u32[]{:S(2)}) copy-start(bf16[2,2,832,128]{3,2,1,0:T(8,128)(2,1)} %param.7) | copy-start | bytes 2555908
  7.2 37.8 %all-gather.5.cloned.1.call-start = ((), (), s32[]{:S(2)}) async-start(), calls=%async_computation | async-start | bytes 1597440 | tf_op jit(solution)/shard_map/all_gather | solution.py:49
  9.7 169.1 %all-gather.7.cloned.1.call-start = ((), (), s32[]{:S(2)}) async-start(), calls=%async_computation.1 | async-start | bytes 11501568 | tf_op jit(solution)/shard_map/all_gather | solution.py:50
  45.1 4.0 %copy-start.9 = (s32[3]{0:T(128)S(1)}, s32[3]{0:T(128)}, u32[]{:S(2)}) copy-start(s32[3]{0:T(128)} %param.11) | copy-start | bytes 40
  45.2 0.8 copy-start.3
  45.2 0.9 copy-start.5
  46.1 3.6 %copy-start.2 = (f32[128]{0:T(128)S(1)}, f32[128]{0:T(128)}, u32[]{:S(2)}) copy-start(f32[128]{0:T(128)} %param.9) | copy-start | bytes 1540
  105.4 3.6 %copy-start.8 = (f32[1536]{0:T(1024)S(1)}, f32[1536]{0:T(1024)}, u32[]{:S(2)}) copy-start(f32[1536]{0:T(1024)} %param.10) | copy-start | bytes 18436
  105.4 3.8 %copy-start.4 = (bf16[2,832,128]{2,1,0:T(8,128)(2,1)S(1)}, bf16[2,832,128]{2,1,0:T(8,128)(2,1)}, u32[]{:S(2)}) copy-start(bf16[2,832,128]{2,1,0:T(8,128)(2,1)} %copy-done.3) | copy-start | bytes 1277956
  109.0 12.0 %collective-permute-start = (bf16[48,3,2,384]{3,0,1,2:T(8,128)(2,1)S(1)}, bf16[48,3,2,384]{3,0,1,2:T(8,128)(2,1)}, u32[]{:S(2)}, u32[]{:S(2)}) collective-permute-start(bf16[48,3,2,384]{3,0,1,2:T(8,128)(2,1)S(1)} %get-tuple-element.23), channel_id=1, source_target_pairs={{0,3},{1,0},{2,1},{3,2},{4,7},{5,4},{6,5},{7,6},{8,11},{9,8},{10,9... | collective-permute-start | bytes 663560 | tf_op jit(solution)/shard_map/ppermute | solution.py:65
  120.9 21.5 %collective-permute-start.1 = (bf16[48,3,2,384]{3,0,1,2:T(8,128)(2,1)}, bf16[48,3,2,384]{3,0,1,2:T(8,128)(2,1)S(1)}, u32[]{:S(2)}, u32[]{:S(2)}) collective-permute-start(bf16[48,3,2,384]{3,0,1,2:T(8,128)(2,1)} %collective-permute-done), channel_id=1, source_target_pairs={{0,3},{1,0},{2,1},{3,2},{4,7},{5,4},{6,5},{7,6},{8,11},{9,8},{10,9... | collective-permute-start | bytes 663560 | tf_op jit(solution)/shard_map/ppermute | solution.py:65
  132.1 14.8 %copy-start.7 = (bf16[48,3,2,3072]{3,0,1,2:T(8,128)(2,1)S(1)}, bf16[48,3,2,3072]{3,0,1,2:T(8,128)(2,1)}, u32[]{:S(2)}) copy-start(bf16[48,3,2,3072]{3,0,1,2:T(8,128)(2,1)} %get-tuple-element.22) | copy-start | bytes 5308420
  142.5 8.3 %collective-permute-start.2 = (bf16[48,3,2,384]{3,0,1,2:T(8,128)(2,1)S(1)}, bf16[48,3,2,384]{3,0,1,2:T(8,128)(2,1)S(1)}, u32[]{:S(2)}, u32[]{:S(2)}) collective-permute-start(bf16[48,3,2,384]{3,0,1,2:T(8,128)(2,1)S(1)} %collective-permute-done.1), channel_id=1, source_target_pairs={{0,3},{1,0},{2,1},{3,2},{4,7},{5,4},{6,5},{7,6},{8,11},{9,8},{10,9... | collective-permute-start | bytes 663560 | tf_op jit(solution)/shard_map/ppermute | solution.py:65
  152.0 2.2 %slice-start = ((s8[5308416]{0:T(1024)(128)(4,1)}), s8[4194304]{0:T(1024)(128)(4,1)S(1)}, s32[]{:S(2)}) async-start(s8[5308416]{0:T(1024)(128)(4,1)} %bitcast.78), calls=%async_computation.2 | async-start | bytes 8388608
  152.1 2.4 %slice-start.1 = ((s8[5308416]{0:T(1024)(128)(4,1)}), s8[1114112]{0:T(1024)(128)(4,1)S(1)}, s32[]{:S(2)}) async-start(s8[5308416]{0:T(1024)(128)(4,1)} %bitcast.78), calls=%async_computation.3 | async-start | bytes 2228224
  191.0 9.1 %copy-start.1 = (bf16[2,2,832,384]{3,2,1,0:T(8,128)(2,1)S(1)}, bf16[2,2,832,384]{3,2,1,0:T(8,128)(2,1)}, u32[]{:S(2)}) copy-start(bf16[2,2,832,384]{3,2,1,0:T(8,128)(2,1)} %param.8) | copy-start | bytes 7667716
Sparse Core Ops, SparseCore 0:
  10.2 34.8 all-gather.4
  46.9 64.6 all-gather.6
